TPU v7x, 256 devices: a whole 4x4x8 slice. The times are simulated.
256 devices in a mesh: row: 16 (over z_hi, y, core), col: 4 (over z_lo), pblk: 4 (over x).
Axes of the slice: x: 4, y: 4, z: 8 (z_hi: 2, z_lo: 4; z = z_hi * 4 + z_lo), core: 2. Of those that a mesh axis runs over, the one named last changes fastest.
Arguments:
- left_feat: int32 [2048, 256], P(('row', 'col', 'pblk')), may hold values from 0 to 255
- right_feat: int32 [4, 4, 64, 256], P('col', 'pblk', 'row'), may hold values from 0 to 255
- embed: bfloat16 [1024, 256], replicated, may hold values from -12 to 12
- conv_w: bfloat16 [8, 768, 256], replicated, may hold values from -0.01953125 to 0.01953125
- head: float32 [256], replicated, may hold values from -0.078125 to 0.078125
- assign: int32 [8], replicated, may hold values from 0 to 3, as said below
- proj_delta: bfloat16 [4, 256, 128], replicated, may hold values from -0.375 to 0.375
- proj_input: bfloat16 [4, 768, 128], replicated, may hold values from -0.21875 to 0.21875
Outputs:
- kernel: float32 [2048, 1024], P('row', ('col', 'pblk'))
Inputs may be any that keep to these rules, and one draw needn't show every extreme that they name: `assign`: every one of the 4 blocks is named by exactly 2 layers.
All inputs are finite; a program needn't handle non-finite values.
Results may differ from a plain program's by a relative error of at most 0.00036.
Values may be sent and summed in bfloat16 or wider, within the bound.
No kernel may reach another device: no remote copies, remote signals or barrier semaphores. Data moves between devices by JAX's collectives and lax.ppermute only.
A program may use at most 128 MiB of HBM per device.

v0:
```python
import jax
import jax.numpy as jnp
from jax import lax
from jax.sharding import Mesh, PartitionSpec as P

SEQ = 64
NFEAT = 4
VOCAB = 256
LAYERS = 8
PR = 128
PS = 128


def shift_wide(inputs):
    blank = jnp.zeros_like(inputs[:, :1])
    earlier = jnp.concatenate([blank, inputs[:, :-1]], 1)
    later_cells = jnp.concatenate([inputs[:, 1:], blank], 1)
    return jnp.concatenate([earlier, inputs, later_cells], 2)


def panels(features, embed, conv_w, head, assign, proj_delta, proj_input):
    examples = features.shape[0]
    blocks_here = proj_delta.shape[0]
    offsets = jnp.arange(NFEAT, dtype=jnp.int32) * VOCAB
    table_rows = features.reshape(examples, SEQ, NFEAT) + offsets
    table_ids = jnp.arange(NFEAT * VOCAB, dtype=jnp.int32)
    onehot = (table_rows[:, :, 0:1] == table_ids).astype(jnp.bfloat16)
    for field in range(1, NFEAT):
        onehot = onehot + (table_rows[:, :, field : field + 1] == table_ids).astype(jnp.bfloat16)
    hidden = jnp.einsum("esv,vc->esc", onehot, embed, preferred_element_type=jnp.float32)
    wides = []
    pres = []
    for layer in range(LAYERS):
        wide_input = shift_wide(hidden.astype(jnp.bfloat16))
        pre_act = jnp.einsum(
            "esk,kc->esc", wide_input, conv_w[layer], preferred_element_type=jnp.float32
        )
        wides.append(wide_input)
        pres.append(pre_act)
        hidden = hidden + jax.nn.silu(pre_act)
    grad_h = jnp.broadcast_to(head / SEQ, hidden.shape)
    block_ids = jnp.arange(blocks_here, dtype=jnp.int32)
    panel = jnp.zeros((examples, blocks_here, PR, PS), jnp.float32)
    for layer in range(LAYERS - 1, -1, -1):
        pre_act = pres[layer]
        sigmoid_z = jax.nn.sigmoid(pre_act)
        delta_low = (grad_h * sigmoid_z * (1.0 + pre_act * (1.0 - sigmoid_z))).astype(jnp.bfloat16)
        block_pick = (assign[layer] == block_ids).astype(jnp.float32)
        rows_table = jnp.einsum("b,bcr->cr", block_pick, proj_delta.astype(jnp.float32)).astype(
            jnp.bfloat16
        )
        cols_table = jnp.einsum("b,bkt->kt", block_pick, proj_input.astype(jnp.float32)).astype(
            jnp.bfloat16
        )
        left_side = jnp.einsum(
            "esc,cr->esr", delta_low, rows_table, preferred_element_type=jnp.float32
        )
        right_side = jnp.einsum(
            "esk,kt->est", wides[layer], cols_table, preferred_element_type=jnp.float32
        )
        projected = jnp.einsum(
            "esr,est->ert", left_side, right_side, precision=lax.Precision.HIGHEST
        )
        panel = panel + block_pick[None, :, None, None] * projected[:, None]
        if layer > 0:
            back_wide = jnp.einsum(
                "esc,kc->esk", delta_low, conv_w[layer], preferred_element_type=jnp.float32
            )
            width = grad_h.shape[2]
            first_third = back_wide[:, :, :width]
            last_third = back_wide[:, :, 2 * width :]
            blank = jnp.zeros_like(first_third[:, :1])
            grad_input = back_wide[:, :, width : 2 * width]
            grad_input = grad_input + jnp.concatenate([first_third[:, 1:], blank], 1)
            grad_input = grad_input + jnp.concatenate([blank, last_third[:, :-1]], 1)
            grad_h = grad_h + grad_input
    return panel.reshape(examples, blocks_here, PR * PS).astype(jnp.bfloat16)


def on_device(left_feat, right_feat, embed, conv_w, head, assign, proj_delta, proj_input):
    group = ("zh", "core", "col")
    n_group = lax.axis_size(group)
    n_zh = lax.axis_size("zh")
    n_core = lax.axis_size("core")
    n_col = lax.axis_size("col")
    n_y = lax.axis_size("y")
    n_blk = lax.axis_size("pblk")
    left_each = left_feat.shape[0]
    right_each = right_feat.shape[2]
    right_local = right_feat.reshape(right_each, right_feat.shape[3])
    own_features = jnp.concatenate([left_feat, right_local], 0)
    panel = panels(own_features, embed, conv_w, head, assign, proj_delta, proj_input)
    own = panel.shape[0]
    width = panel.shape[1] * panel.shape[2] // n_group
    sliced = panel.reshape(own, n_group, width)
    spread = lax.all_to_all(sliced, group, split_axis=1, concat_axis=0, tiled=True)
    spread = spread.reshape(n_group, own, width)
    left_part = spread[:, :left_each].reshape(n_group * left_each, width)
    right_part = spread[:, left_each:].reshape(n_group * right_each, width)
    left_tile = lax.all_gather(left_part, "pblk", axis=0, tiled=True)
    right_tile = lax.all_gather(right_part, "y", axis=0, tiled=True)
    partial_tile = jnp.einsum(
        "lk,rk->lr", left_tile, right_tile, preferred_element_type=jnp.float32
    )
    partial_tile = partial_tile.reshape(
        n_blk, n_zh, n_core, n_col, left_each, n_y, n_zh, n_core, n_col, right_each
    )
    chunks = jnp.transpose(partial_tile, (1, 2, 8, 3, 0, 4, 6, 5, 7, 9))
    chunks = chunks.reshape(n_group, n_col * n_blk * left_each, n_zh * n_y * n_core * right_each)
    block = lax.psum_scatter(chunks, group, scatter_dimension=0, tiled=True)
    return block.reshape(block.shape[1], block.shape[2])


def solution(mesh):
    n_row = mesh.shape["row"]
    fine = Mesh(
        mesh.devices.reshape(2, 4, n_row // 8, mesh.shape["col"], mesh.shape["pblk"]),
        ("zh", "y", "core", "col", "pblk"),
    )
    rows = ("zh", "y", "core")
    placed = (
        P((*rows, "col", "pblk"), None),
        P("col", "pblk", rows, None),
        P(),
        P(),
        P(),
        P(),
        P(),
        P(),
    )
    return jax.shard_map(
        on_device, mesh=fine, in_specs=placed, out_specs=P(rows, ("col", "pblk")), check_vma=False
    )
```

profile of v0, /device:TPU:1, one launch (start us, length us, event | category | flops | bytes accessed | tf_op | source)
XLA Modules:
  0.0 414.9 jit_solution(5127504593989071444)
XLA Ops:
  6.5 1.6 fusion.261
  22.4 1.9 fusion.159
  24.2 2.0 fusion.163
  26.2 1.9 fusion.167
  28.1 2.0 fusion.171
  30.1 2.0 fusion.175
  37.8 2.8 fusion.262
  85.2 2.4 mul.370
  87.6 5.2 %mul.371 = f32[12,16,4096]{2,1,0:T(8,128)} reshape(f32[12,4,16384]{2,1,0:T(4,128)} %mul.370) | data formatting | bytes 6291456 | tf_op jit(solution)/shard_map/mul | solution.py:64
  92.8 3.7 mul.360
  96.5 5.2 %mul.361 = f32[12,16,4096]{2,1,0:T(8,128)} reshape(f32[12,4,16384]{2,1,0:T(4,128)} %mul.360) | data formatting | bytes 6291456 | tf_op jit(solution)/shard_map/mul | solution.py:64
  101.7 3.7 mul.350
  105.4 5.4 %mul.351 = f32[12,16,4096]{2,1,0:T(8,128)} reshape(f32[12,4,16384]{2,1,0:T(4,128)} %mul.350) | data formatting | bytes 6291456 | tf_op jit(solution)/shard_map/mul | solution.py:64
  110.8 3.6 mul.340
  114.4 5.3 %mul.341 = f32[12,16,4096]{2,1,0:T(8,128)} reshape(f32[12,4,16384]{2,1,0:T(4,128)} %mul.340) | data formatting | bytes 6291456 | tf_op jit(solution)/shard_map/mul | solution.py:64
  119.7 3.6 mul.330
  123.3 5.3 %mul.331 = f32[12,16,4096]{2,1,0:T(8,128)} reshape(f32[12,4,16384]{2,1,0:T(4,128)} %mul.330) | data formatting | bytes 6291456 | tf_op jit(solution)/shard_map/mul | solution.py:64
  128.6 3.7 mul.320
  132.2 5.2 %mul.321 = f32[12,16,4096]{2,1,0:T(8,128)} reshape(f32[12,4,16384]{2,1,0:T(4,128)} %mul.320) | data formatting | bytes 6291456 | tf_op jit(solution)/shard_map/mul | solution.py:64
  137.5 2.4 mul.310
  139.9 5.2 %mul.311 = f32[12,16,4096]{2,1,0:T(8,128)} reshape(f32[12,4,16384]{2,1,0:T(4,128)} %mul.310) | data formatting | bytes 6291456 | tf_op jit(solution)/shard_map/mul | solution.py:64
  145.2 2.4 mul.300
  147.5 5.3 %mul.301 = f32[12,16,4096]{2,1,0:T(8,128)} reshape(f32[12,4,16384]{2,1,0:T(4,128)} %mul.300) | data formatting | bytes 6291456 | tf_op jit(solution)/shard_map/mul | solution.py:64
  152.8 9.6 %add_convert_fusion = bf16[12,16,4096]{2,1,0:T(8,128)(2,1)S(1)} fusion(f32[12,16,4096]{2,1,0:T(8,128)} %mul.371, f32[12,16,4096]{2,1,0:T(8,128)} %mul.361, f32[12,16,4096]{2,1,0:T(8,128)} %mul.351, f32[12,16,4096]{2,1,0:T(8,128)} %mul.341, f32[12,16,4096]{2,1,0:T(8,128)} %mul.331, f32[12,16,4096]{2,1,0:T(8,128)} %mul.321, f32[12,16,4096]{2,1,0:T(8,128)} %mul.311, ...), kind=kLoop, calls=%fused_computation | loop fusion | flops 12582912 | bytes 26739200 | tf_op jit(solution)/shard_map/convert_element_type | solution.py:77
  163.3 57.9 %all_to_all.15 = bf16[12,16,4096]{2,0,1:T(8,128)(2,1)S(1)} all-to-all(bf16[12,16,4096]{2,0,1:T(8,128)(2,1)S(1)} %copy.40), channel_id=1, replica_groups=mesh['zh'=2,'y'=4,'core'=2,'col'=4,'pblk'=4] {'zh','core','col'}, dimensions={1} | all-to-all | bytes 3145728 | tf_op jit(solution)/shard_map/all_to_all | solution.py:96
  223.6 31.7 %all-gather.5.cloned.1.call-done = bf16[256,4096]{1,0:T(8,128)(2,1)} async-done(((bf16[64,4096]{1,0:T(8,128)(2,1)}), bf16[256,4096]{1,0:T(8,128)(2,1)}) %all-gather.5.cloned.1.call-update) | async-done | bytes 2097168 | tf_op jit(solution)/shard_map/all_gather | solution.py:101
  255.3 52.6 %all-gather.3.cloned.1.call-done = bf16[512,4096]{1,0:T(8,128)(2,1)} async-done(((bf16[128,4096]{1,0:T(8,128)(2,1)}), bf16[512,4096]{1,0:T(8,128)(2,1)}) %all-gather.3.cloned.1.call-update) | async-done | bytes 4194320 | tf_op jit(solution)/shard_map/all_gather | solution.py:100
  307.9 4.2 %fusion.271 = f32[512,256]{0,1:T(8,128)S(1)} fusion(bf16[512,4096]{1,0:T(8,128)(2,1)} %all-gather.3.cloned.1.call-done, bf16[256,4096]{1,0:T(8,128)(2,1)} %all-gather.5.cloned.1.call-done), kind=kOutput, calls=%fused_computation.291 | convolution fusion | flops 1073741824 | bytes 6815744 | tf_op jit(solution)/shard_map/lk,rk->lr/dot_general | solution.py:102
  312.1 11.5 %reshape.113 = f32[4,2,2,4,8,4,2,2,4,4]{4,3,2,1,0,9,8,7,6,5:T(4,128)} reshape(f32[512,256]{0,1:T(8,128)S(1)} %fusion.271) | data formatting | bytes 1048576 | tf_op jit(solution)/shard_map/reshape | solution.py:105
  323.6 9.9 %copy.42 = f32[2,2,4,4,4,8,2,4,2,4]{5,4,3,9,8,7,6,2,1,0:T(4,128)} copy(f32[2,2,4,4,4,8,2,4,2,4]{5,3,1,0,4,9,2,8,6,7:T(4,128)} %bitcast.292) | data formatting | bytes 1048576 | tf_op jit(solution)/shard_map/transpose | solution.py:108
  333.5 11.1 %reshape.114 = f32[16,128,64]{1,2,0:T(8,128)} reshape(f32[2,2,4,4,4,8,2,4,2,4]{5,4,3,9,8,7,6,2,1,0:T(4,128)} %copy.42) | data formatting | bytes 1048576 | tf_op jit(solution)/shard_map/reshape | solution.py:109
  344.6 63.3 %reduce-scatter.2.cloned.1.call-done = f32[1,128,64]{1,2,0:T(8,128)} async-done(((f32[16,128,64]{1,2,0:T(8,128)}), f32[1,128,64]{1,2,0:T(8,128)}) %reduce-scatter.2.cloned.1.call-update) | async-done | bytes 32784 | tf_op jit(solution)/shard_map/reduce_scatter | solution.py:110
  (157 shorter events, 67.0 us)
Async XLA Ops:
  6.5 31.3 %copy-start = (bf16[1024,256]{1,0:T(8,128)(2,1)S(1)}, bf16[1024,256]{1,0:T(8,128)(2,1)}, u32[]{:S(2)}) copy-start(bf16[1024,256]{1,0:T(8,128)(2,1)} %param.10) | copy-start | bytes 1572868
  6.5 15.2 %copy-start.3 = (bf16[4,768,128]{2,1,0:T(8,128)(2,1)S(1)}, bf16[4,768,128]{2,1,0:T(8,128)(2,1)}, u32[]{:S(2)}) copy-start(bf16[4,768,128]{2,1,0:T(8,128)(2,1)} %param.15) | copy-start | bytes 2359300
  6.5 248.8 %all-gather.5.cloned.1.call-start = ((), (), s32[]{:S(2)}) async-start(), calls=%async_computation.3 | async-start | bytes 2621440 | tf_op jit(solution)/shard_map/all_gather | solution.py:101
  32.1 3.6 copy-start.6
  32.1 4.8 %copy-start.4 = (s32[8,256]{1,0:T(8,128)S(1)}, s32[8,256]{1,0:T(8,128)}, u32[]{:S(2)}) copy-start(s32[8,256]{1,0:T(8,128)} %param.8) | copy-start | bytes 24580
  32.1 5.0 %copy-start.5 = (s32[1,1,4,256]{3,2,1,0:T(4,128)S(1)}, s32[1,1,4,256]{3,2,1,0:T(4,128)}, u32[]{:S(2)}) copy-start(s32[1,1,4,256]{3,2,1,0:T(4,128)} %param.9) | copy-start | bytes 12292
  37.8 3.0 copy-start.11
  40.8 1.9 copy-start.2
  42.7 1.0 copy-start.10
  44.2 1.0 copy-start.9
  45.6 1.0 copy-start.8
  47.1 1.0 copy-start.7
  222.5 85.5 %all-gather.3.cloned.1.call-start = ((), (), s32[]{:S(2)}) async-start(), calls=%async_computation.2 | async-start | bytes 5242880 | tf_op jit(solution)/shard_map/all_gather | solution.py:100
  223.6 184.3 %reduce-scatter.2.cloned.1.call-start = ((), (), s32[]{:S(2)}) async-start(), calls=%async_computation.4 | async-start | bytes 557056 | tf_op jit(solution)/shard_map/reduce_scatter | solution.py:110
  333.5 74.4 %copy-start.1 = (bf16[1024,256]{1,0:T(8,128)(2,1)S(1)}, bf16[1024,256]{1,0:T(8,128)(2,1)}, u32[]{:S(2)}) copy-start(bf16[1024,256]{1,0:T(8,128)(2,1)} %param.10) | copy-start | bytes 1572868
Sparse Core Ops, SparseCore 0:
  222.6 32.7 all-gather.4
  257.1 50.7 all-gather.2
  344.8 63.1 reduce-scatter.1
where the time goes:
time: 422 us; the launch traced here: 415 us
  waiting for transfers between devices  148 us (35%)
  local copies, waits for them, and re-layouts  124 us (29%)
  blocking collectives  57.9 us (14%)
  matrix products  53.7 us (13%)
  other arithmetic  17.5 us (4%)
  between operations  14.3 us (3%)
    mul x32, local copies, waits for them, and re-layouts, panels(): panel = panel + block_pick[None, :, None, None] * projected[:, None]  68.9 us
    reduce_scatter x1, waiting for transfers between devices, on_device(): block = lax.psum_scatter(chunks, group, scatter_dimension=0, tiled=True)  63.3 us
    all_to_all x1, blocking collectives, on_device(): lax.all_to_all(sliced, group, split_axis=1, concat_axis=0, tiled=True)  57.9 us
    all_gather x1, waiting for transfers between devices, on_device(): left_tile = lax.all_gather(left_part, 'pblk', axis=0, tiled=True)  52.6 us
    all_gather x1, waiting for transfers between devices, on_device(): right_tile = lax.all_gather(right_part, 'y', axis=0, tiled=True)  31.7 us
    unnamed x43, local copies, waits for them, and re-layouts  14.8 us
    dot_general x8, matrix products, panels(): jnp.einsum('b,bkt->kt', block_pick, proj_input.astype(jnp.float32))  13.3 us
    reshape x1, local copies, waits for them, and re-layouts, on_device(): partial_tile.reshape(n_blk, n_zh, n_core, n_col, left_each, n_y, n_zh, n_...  11.5 us
  transfers between devices with their start and end apart: 3, of which 3 were waited for; matrix products, arithmetic and copies ran while one was open for 0% of the time, Pallas kernels for 0%

commit v1 on v0

--- a/solution.py
+++ b/solution.py
@@ -97,10 +97,47 @@
     spread = spread.reshape(n_group, own, width)
     left_part = spread[:, :left_each].reshape(n_group * left_each, width)
     right_part = spread[:, left_each:].reshape(n_group * right_each, width)
-    left_tile = lax.all_gather(left_part, "pblk", axis=0, tiled=True)
     right_tile = lax.all_gather(right_part, "y", axis=0, tiled=True)
-    partial_tile = jnp.einsum(
-        "lk,rk->lr", left_tile, right_tile, preferred_element_type=jnp.float32
+
+    def get_arrays(chunk, dev_axis, sample):
+        oldest, vec_out, reply = (
+            jax.lax.axis_size(dev_axis),
+            jax.lax.axis_index(dev_axis),
+            chunk.shape[0],
+        )
+        sheets = [(dev, (dev + 1) % oldest) for dev in range(oldest)]
+        column = [(j, idx) for idx, j in sheets]
+        state_next, w1 = (
+            jax.lax.ppermute(chunk, dev_axis, sheets),
+            jax.lax.ppermute(chunk, dev_axis, column),
+        )
+        v1 = sample(chunk, vec_out * reply)
+        inter = v1.shape[0]
+        new = jnp.zeros((*v1.shape[:0], oldest * inter, *v1.shape[1:]), v1.dtype)
+
+        def _track_block(new, v1, prior):
+            return lax.dynamic_update_slice_in_dim(new, v1, prior * inter, axis=0)
+
+        new = _track_block(new, v1, vec_out)
+        for at in tuple(range(1, oldest // 2 + 1)):
+            after, spare = ((vec_out - at) % oldest, (vec_out + at) % oldest)
+            state_now = (state_next, w1)
+            if at < oldest // 2:
+                state_next, w1 = (
+                    jax.lax.ppermute(state_next, dev_axis, sheets),
+                    jax.lax.ppermute(w1, dev_axis, column),
+                )
+            new = _track_block(new, sample(state_now[0], after * reply), after)
+            if 2 * at < oldest:
+                new = _track_block(new, sample(state_now[1], spare * reply), spare)
+        return new
+
+    partial_tile = get_arrays(
+        left_part,
+        "pblk",
+        lambda own_block, start: jnp.einsum(
+            "lk,rk->lr", own_block, right_tile, preferred_element_type=jnp.float32
+        ),
     )
     partial_tile = partial_tile.reshape(
         n_blk, n_zh, n_core, n_col, left_each, n_y, n_zh, n_core, n_col, right_each

time: 422 us -> 391 us (0.927)
  waiting for transfers between devices: 148 us -> 104 us
  matrix products: 53.7 us -> 69.4 us
  local copies, waits for them, and re-layouts: 124 us -> 115 us
    all_gather x1 -> x0, waiting for transfers between devices: 52.6 us -> none  [on_device(): left_tile = lax.all_gather(left_part, 'pblk', axis=0, tiled=True)]
    ppermute x0 -> x3, waiting for transfers between devices: none -> 35.7 us  [the longest x1 23 us: get_arrays(): jax.lax.ppermute(chunk, dev_axis, sheets)]
    all_gather x1, waiting for transfers between devices: 31.7 us -> 5.86 us  [on_device(): right_tile = lax.all_gather(right_part, 'y', axis=0, tiled=True)]
    dot_general x8, matrix products: 3.85 us -> 9.74 us  [panels(): jnp.einsum('esk,kt->est', wides[layer], cols_table, preferred_element_typ...]
    mul x32, local copies, waits for them, and re-layouts: 68.9 us -> 63.5 us  [panels(): panel = panel + block_pick[None, :, None, None] * projected[:, None]]
    unnamed x43 -> x123, local copies, waits for them, and re-layouts: 14.8 us -> 11.9 us
  transfers between devices with their start and end apart: 3 -> 5, of which waited for: 3 -> 4; matrix products, arithmetic and copies ran while one was open for 0% -> 2% of each run, Pallas kernels for 0% -> 0%
where the time goes in v1:
time: 391 us; the launch traced here: 383 us
  local copies, waits for them, and re-layouts  115 us (29%)
  waiting for transfers between devices  104 us (27%)
  matrix products  69.4 us (18%)
  blocking collectives  57.9 us (15%)
  other arithmetic  19.3 us (5%)
  between operations  14.9 us (4%)
    mul x32, local copies, waits for them, and re-layouts, panels(): panel = panel + block_pick[None, :, None, None] * projected[:, None]  63.5 us
    reduce_scatter x1, waiting for transfers between devices, on_device(): block = lax.psum_scatter(chunks, group, scatter_dimension=0, tiled=True)  62 us
    all_to_all x1, blocking collectives, on_device(): lax.all_to_all(sliced, group, split_axis=1, concat_axis=0, tiled=True)  57.9 us
    ppermute x1, waiting for transfers between devices, get_arrays(): jax.lax.ppermute(chunk, dev_axis, sheets)  23 us
    dot_general x8, matrix products, panels(): jnp.einsum('b,bkt->kt', block_pick, proj_input.astype(jnp.float32))  15.3 us
    ppermute x1, waiting for transfers between devices, get_arrays(): jax.lax.ppermute(state_next, dev_axis, sheets)  12.7 us
    unnamed x123, local copies, waits for them, and re-layouts  11.9 us
    dot_general x8, matrix products, panels(): jnp.einsum('esr,est->ert', left_side, right_side, precision=lax.Precision...  11.3 us
  transfers between devices with their start and end apart: 5, of which 4 were waited for; matrix products, arithmetic and copies ran while one was open for 2% of the time, Pallas kernels for 0%

profile of v1, /device:TPU:1, one launch (start us, length us, event | category | flops | bytes accessed | tf_op | source)
XLA Modules:
  0.0 383.5 jit_solution(16439235554031140274)
XLA Ops:
  19.4 2.0 fusion.167
  29.8 1.9 fusion.179
  35.5 2.0 fusion.187
  45.3 2.8 fusion.262
  68.4 2.4 mul.382
  70.9 5.2 %mul.383 = f32[12,16,4096]{2,1,0:T(8,128)} reshape(f32[12,4,16384]{2,1,0:T(4,128)} %mul.382) | data formatting | bytes 6291456 | tf_op jit(solution)/shard_map/mul | solution.py:64
  80.3 2.5 mul.372
  82.8 5.3 %mul.373 = f32[12,16,4096]{2,1,0:T(8,128)} reshape(f32[12,4,16384]{2,1,0:T(4,128)} %mul.372) | data formatting | bytes 6291456 | tf_op jit(solution)/shard_map/mul | solution.py:64
  92.2 2.5 mul.362
  94.7 5.4 %mul.363 = f32[12,16,4096]{2,1,0:T(8,128)} reshape(f32[12,4,16384]{2,1,0:T(4,128)} %mul.362) | data formatting | bytes 6291456 | tf_op jit(solution)/shard_map/mul | solution.py:64
  104.3 2.4 mul.352
  106.7 5.4 %mul.353 = f32[12,16,4096]{2,1,0:T(8,128)} reshape(f32[12,4,16384]{2,1,0:T(4,128)} %mul.352) | data formatting | bytes 6291456 | tf_op jit(solution)/shard_map/mul | solution.py:64
  116.1 2.4 mul.342
  118.4 5.3 %mul.343 = f32[12,16,4096]{2,1,0:T(8,128)} reshape(f32[12,4,16384]{2,1,0:T(4,128)} %mul.342) | data formatting | bytes 6291456 | tf_op jit(solution)/shard_map/mul | solution.py:64
  127.7 2.4 mul.332
  130.1 5.5 %mul.333 = f32[12,16,4096]{2,1,0:T(8,128)} reshape(f32[12,4,16384]{2,1,0:T(4,128)} %mul.332) | data formatting | bytes 6291456 | tf_op jit(solution)/shard_map/mul | solution.py:64
  138.5 2.5 mul.322
  141.0 5.3 %mul.323 = f32[12,16,4096]{2,1,0:T(8,128)} reshape(f32[12,4,16384]{2,1,0:T(4,128)} %mul.322) | data formatting | bytes 6291456 | tf_op jit(solution)/shard_map/mul | solution.py:64
  149.2 2.4 mul.312
  151.7 5.3 %mul.313 = f32[12,16,4096]{2,1,0:T(8,128)} reshape(f32[12,4,16384]{2,1,0:T(4,128)} %mul.312) | data formatting | bytes 6291456 | tf_op jit(solution)/shard_map/mul | solution.py:64
  158.2 9.6 %add_convert_fusion = bf16[12,16,4096]{2,1,0:T(8,128)(2,1)S(1)} fusion(f32[12,16,4096]{2,1,0:T(8,128)} %mul.383, f32[12,16,4096]{2,1,0:T(8,128)} %mul.373, f32[12,16,4096]{2,1,0:T(8,128)} %mul.363, f32[12,16,4096]{2,1,0:T(8,128)} %mul.353, f32[12,16,4096]{2,1,0:T(8,128)} %mul.343, f32[12,16,4096]{2,1,0:T(8,128)} %mul.333, f32[12,16,4096]{2,1,0:T(8,128)} %mul.323, ...), kind=kLoop, calls=%fused_computation | loop fusion | flops 12582912 | bytes 26739200 | tf_op jit(solution)/shard_map/convert_element_type | solution.py:77
  168.8 57.9 %all_to_all.15 = bf16[12,16,4096]{2,0,1:T(8,128)(2,1)S(1)} all-to-all(bf16[12,16,4096]{2,0,1:T(8,128)(2,1)S(1)} %copy.48), channel_id=1, replica_groups=mesh['zh'=2,'y'=4,'core'=2,'col'=4,'pblk'=4] {'zh','core','col'}, dimensions={1} | all-to-all | bytes 3145728 | tf_op jit(solution)/shard_map/all_to_all | solution.py:96
  231.9 23.0 %collective-permute-done = bf16[128,4096]{1,0:T(8,128)(2,1)} collective-permute-done((bf16[128,4096]{1,0:T(8,128)(2,1)}, bf16[128,4096]{1,0:T(8,128)(2,1)}, u32[]{:S(2)}, u32[]{:S(2)}) %collective-permute-start) | collective-permute-done | bytes 1048608 | tf_op jit(solution)/shard_map/ppermute | solution.py:111
  254.9 5.9 %all-gather.2.cloned.1.call-done = bf16[256,4096]{1,0:T(8,128)(2,1)} async-done(((bf16[64,4096]{1,0:T(8,128)(2,1)}), bf16[256,4096]{1,0:T(8,128)(2,1)}) %all-gather.2.cloned.1.call-update) | async-done | bytes 2097168 | tf_op jit(solution)/shard_map/all_gather | solution.py:100
  260.8 2.4 convolution_dynamic-update-slice_fusion.3
  263.2 1.9 convolution_dynamic-update-slice_fusion.2
  265.2 1.9 convolution_dynamic-update-slice_fusion.1
  267.1 12.7 %collective-permute-done.2 = bf16[128,4096]{1,0:T(8,128)(2,1)} collective-permute-done((bf16[128,4096]{1,0:T(8,128)(2,1)}, bf16[128,4096]{1,0:T(8,128)(2,1)}, u32[]{:S(2)}, u32[]{:S(2)}) %collective-permute-start.2) | collective-permute-done | bytes 1048608 | tf_op jit(solution)/shard_map/ppermute | solution.py:127
  281.8 11.3 %reshape.113 = f32[4,2,2,4,8,4,2,2,4,4]{4,3,2,1,0,9,8,7,6,5:T(4,128)} reshape(f32[512,256]{0,1:T(8,128)S(1)} %convolution_dynamic-update-slice_fusion) | data formatting | bytes 1048576 | tf_op jit(solution)/shard_map/reshape | solution.py:142
  293.1 10.0 %copy.53 = f32[2,2,4,4,4,8,2,4,2,4]{5,4,3,9,8,7,6,2,1,0:T(4,128)} copy(f32[2,2,4,4,4,8,2,4,2,4]{5,3,1,0,4,9,2,8,6,7:T(4,128)} %bitcast.298) | data formatting | bytes 1048576 | tf_op jit(solution)/shard_map/transpose | solution.py:145
  303.1 11.1 %reshape.114 = f32[16,128,64]{1,2,0:T(8,128)} reshape(f32[2,2,4,4,4,8,2,4,2,4]{5,4,3,9,8,7,6,2,1,0:T(4,128)} %copy.53) | data formatting | bytes 1048576 | tf_op jit(solution)/shard_map/reshape | solution.py:146
  314.2 62.0 %reduce-scatter.2.cloned.1.call-done = f32[1,128,64]{1,2,0:T(8,128)} async-done(((f32[16,128,64]{1,2,0:T(8,128)}), f32[1,128,64]{1,2,0:T(8,128)}) %reduce-scatter.2.cloned.1.call-update) | async-done | bytes 32784 | tf_op jit(solution)/shard_map/reduce_scatter | solution.py:147
  (244 shorter events, 87.8 us)
Async XLA Ops:
  6.5 38.7 %copy-start = (bf16[1024,256]{1,0:T(8,128)(2,1)S(1)}, bf16[1024,256]{1,0:T(8,128)(2,1)}, u32[]{:S(2)}) copy-start(bf16[1024,256]{1,0:T(8,128)(2,1)} %param.10) | copy-start | bytes 1572868
  6.5 254.2 %all-gather.2.cloned.1.call-start = ((), (), s32[]{:S(2)}) async-start(), calls=%async_computation.2 | async-start | bytes 2621440 | tf_op jit(solution)/shard_map/all_gather | solution.py:100
  31.8 12.6 %copy-start.42 = (s32[1,1,4,256]{3,2,1,0:T(4,128)S(1)}, s32[1,1,4,256]{3,2,1,0:T(4,128)}, u32[]{:S(2)}) copy-start(s32[1,1,4,256]{3,2,1,0:T(4,128)} %param.9) | copy-start | bytes 12292
  31.8 12.8 %copy-start.41 = (s32[8,256]{1,0:T(8,128)S(1)}, s32[8,256]{1,0:T(8,128)}, u32[]{:S(2)}) copy-start(s32[8,256]{1,0:T(8,128)} %param.8) | copy-start | bytes 24580
  70.9 5.2 %copy-start.40 = (f32[1,256,128]{2,0,1:T(1,128)S(1)}, f32[1,256,128]{2,0,1:T(1,128)}, u32[]{:S(2)}) copy-start(f32[1,256,128]{2,0,1:T(1,128)} %fusion.165) | copy-start | bytes 393220
  82.8 5.3 %copy-start.39 = (f32[1,256,128]{2,0,1:T(1,128)S(1)}, f32[1,256,128]{2,0,1:T(1,128)}, u32[]{:S(2)}) copy-start(f32[1,256,128]{2,0,1:T(1,128)} %fusion.169) | copy-start | bytes 393220
  82.8 5.5 %copy-start.13 = (bf16[12,64,256]{2,1,0:T(8,128)(2,1)S(1)}, bf16[12,64,256]{2,1,0:T(8,128)(2,1)}, u32[]{:S(2)}) copy-start(bf16[12,64,256]{2,1,0:T(8,128)(2,1)} %copy-done.12) | copy-start | bytes 1179652
  94.7 5.5 %copy-start.38 = (f32[1,256,128]{2,0,1:T(1,128)S(1)}, f32[1,256,128]{2,0,1:T(1,128)}, u32[]{:S(2)}) copy-start(f32[1,256,128]{2,0,1:T(1,128)} %fusion.173) | copy-start | bytes 393220
  94.7 5.7 %copy-start.11 = (bf16[12,64,256]{2,1,0:T(8,128)(2,1)S(1)}, bf16[12,64,256]{2,1,0:T(8,128)(2,1)}, u32[]{:S(2)}) copy-start(bf16[12,64,256]{2,1,0:T(8,128)(2,1)} %copy-done.10) | copy-start | bytes 1179652
  106.7 5.4 %copy-start.37 = (f32[1,256,128]{2,0,1:T(1,128)S(1)}, f32[1,256,128]{2,0,1:T(1,128)}, u32[]{:S(2)}) copy-start(f32[1,256,128]{2,0,1:T(1,128)} %fusion.177) | copy-start | bytes 393220
  106.7 5.6 %copy-start.9 = (bf16[12,64,256]{2,1,0:T(8,128)(2,1)S(1)}, bf16[12,64,256]{2,1,0:T(8,128)(2,1)}, u32[]{:S(2)}) copy-start(bf16[12,64,256]{2,1,0:T(8,128)(2,1)} %copy-done.8) | copy-start | bytes 1179652
  106.7 5.6 %copy-start.28 = (bf16[12,63,256]{2,1,0:T(8,128)(2,1)S(1)}, bf16[12,63,256]{2,1,0:T(8,128)(2,1)}, u32[]{:S(2)}) copy-start(bf16[12,63,256]{2,1,0:T(8,128)(2,1)} %copy-done.27) | copy-start | bytes 1161220
  118.4 5.3 %copy-start.36 = (f32[1,256,128]{2,0,1:T(1,128)S(1)}, f32[1,256,128]{2,0,1:T(1,128)}, u32[]{:S(2)}) copy-start(f32[1,256,128]{2,0,1:T(1,128)} %fusion.181) | copy-start | bytes 393220
  118.4 5.6 %copy-start.7 = (bf16[12,64,256]{2,1,0:T(8,128)(2,1)S(1)}, bf16[12,64,256]{2,1,0:T(8,128)(2,1)}, u32[]{:S(2)}) copy-start(bf16[12,64,256]{2,1,0:T(8,128)(2,1)} %copy-done.6) | copy-start | bytes 1179652
  118.4 5.6 %copy-start.24 = (bf16[12,63,256]{2,1,0:T(8,128)(2,1)S(1)}, bf16[12,63,256]{2,1,0:T(8,128)(2,1)}, u32[]{:S(2)}) copy-start(bf16[12,63,256]{2,1,0:T(8,128)(2,1)} %copy-done.23) | copy-start | bytes 1161220
  118.4 5.6 %copy-start.26 = (bf16[12,63,256]{2,1,0:T(8,128)(2,1)S(1)}, bf16[12,63,256]{2,1,0:T(8,128)(2,1)}, u32[]{:S(2)}) copy-start(bf16[12,63,256]{2,1,0:T(8,128)(2,1)} %copy-done.25) | copy-start | bytes 1161220
  130.1 5.8 %copy-start.5 = (bf16[12,64,256]{2,1,0:T(8,128)(2,1)S(1)}, bf16[12,64,256]{2,1,0:T(8,128)(2,1)}, u32[]{:S(2)}) copy-start(bf16[12,64,256]{2,1,0:T(8,128)(2,1)} %copy-done.4) | copy-start | bytes 1179652
  130.1 5.8 %copy-start.20 = (bf16[12,63,256]{2,1,0:T(8,128)(2,1)S(1)}, bf16[12,63,256]{2,1,0:T(8,128)(2,1)}, u32[]{:S(2)}) copy-start(bf16[12,63,256]{2,1,0:T(8,128)(2,1)} %copy-done.19) | copy-start | bytes 1161220
  130.1 5.8 %copy-start.22 = (bf16[12,63,256]{2,1,0:T(8,128)(2,1)S(1)}, bf16[12,63,256]{2,1,0:T(8,128)(2,1)}, u32[]{:S(2)}) copy-start(bf16[12,63,256]{2,1,0:T(8,128)(2,1)} %copy-done.21) | copy-start | bytes 1161220
  130.1 5.9 %copy-start.49 = (f32[1,768,128]{2,0,1:T(1,128)S(1)}, f32[1,768,128]{2,0,1:T(1,128)}, u32[]{:S(2)}) copy-start(f32[1,768,128]{2,0,1:T(1,128)} %fusion.183) | copy-start | bytes 1179652
  141.0 5.6 %copy-start.16 = (bf16[12,63,256]{2,1,0:T(8,128)(2,1)S(1)}, bf16[12,63,256]{2,1,0:T(8,128)(2,1)}, u32[]{:S(2)}) copy-start(bf16[12,63,256]{2,1,0:T(8,128)(2,1)} %copy-done.15) | copy-start | bytes 1161220
  141.0 5.6 %copy-start.18 = (bf16[12,63,256]{2,1,0:T(8,128)(2,1)S(1)}, bf16[12,63,256]{2,1,0:T(8,128)(2,1)}, u32[]{:S(2)}) copy-start(bf16[12,63,256]{2,1,0:T(8,128)(2,1)} %copy-done.17) | copy-start | bytes 1161220
  141.0 5.6 %copy-start.48 = (f32[1,768,128]{2,0,1:T(1,128)S(1)}, f32[1,768,128]{2,0,1:T(1,128)}, u32[]{:S(2)}) copy-start(f32[1,768,128]{2,0,1:T(1,128)} %fusion.187) | copy-start | bytes 1179652
  151.7 5.3 %copy-start.47 = (f32[4]{0:T(128)S(1)}, f32[4]{0:T(128)}, u32[]{:S(2)}) copy-start(f32[4]{0:T(128)} %fusion.191) | copy-start | bytes 52
  151.7 5.5 %copy-start.46 = (f32[4]{0:T(128)S(1)}, f32[4]{0:T(128)}, u32[]{:S(2)}) copy-start(f32[4]{0:T(128)} %fusion.192) | copy-start | bytes 52
  151.7 5.7 %copy-start.45 = (f32[4]{0:T(128)S(1)}, f32[4]{0:T(128)}, u32[]{:S(2)}) copy-start(f32[4]{0:T(128)} %fusion.193) | copy-start | bytes 52
  151.7 5.8 %copy-start.44 = (f32[4]{0:T(128)S(1)}, f32[4]{0:T(128)}, u32[]{:S(2)}) copy-start(f32[4]{0:T(128)} %fusion.194) | copy-start | bytes 52
  227.9 148.3 %reduce-scatter.2.cloned.1.call-start = ((), (), s32[]{:S(2)}) async-start(), calls=%async_computation.3 | async-start | bytes 557056 | tf_op jit(solution)/shard_map/reduce_scatter | solution.py:147
  229.0 25.9 %collective-permute-start = (bf16[128,4096]{1,0:T(8,128)(2,1)}, bf16[128,4096]{1,0:T(8,128)(2,1)}, u32[]{:S(2)}, u32[]{:S(2)}) collective-permute-start(bf16[128,4096]{1,0:T(8,128)(2,1)} %slice_bitcast_fusion), channel_id=1, source_target_pairs={{0,1},{1,2},{2,3},{3,0},{4,5},{5,6},{6,7},{7,4},{8,9},{9,10},{10,1... | collective-permute-start | bytes 3145736 | tf_op jit(solution)/shard_map/ppermute | solution.py:111
  230.2 35.0 %collective-permute-start.1 = (bf16[128,4096]{1,0:T(8,128)(2,1)}, bf16[128,4096]{1,0:T(8,128)(2,1)}, u32[]{:S(2)}, u32[]{:S(2)}) collective-permute-start(bf16[128,4096]{1,0:T(8,128)(2,1)} %slice_bitcast_fusion), channel_id=1, source_target_pairs={{1,0},{2,1},{3,2},{0,3},{5,4},{6,5},{7,6},{4,7},{9,8},{10,9},{11,1... | collective-permute-start | bytes 3145736 | tf_op jit(solution)/shard_map/ppermute | solution.py:112
  254.9 25.0 %collective-permute-start.2 = (bf16[128,4096]{1,0:T(8,128)(2,1)}, bf16[128,4096]{1,0:T(8,128)(2,1)}, u32[]{:S(2)}, u32[]{:S(2)}) collective-permute-start(bf16[128,4096]{1,0:T(8,128)(2,1)} %collective-permute-done), channel_id=1, source_target_pairs={{0,1},{1,2},{2,3},{3,0},{4,5},{5,6},{6,7},{7,4},{8,9},{9,10},{10,1... | collective-permute-start | bytes 3145736 | tf_op jit(solution)/shard_map/ppermute | solution.py:127
  303.1 73.1 %copy-start.1 = (bf16[1024,256]{1,0:T(8,128)(2,1)S(1)}, bf16[1024,256]{1,0:T(8,128)(2,1)}, u32[]{:S(2)}) copy-start(bf16[1024,256]{1,0:T(8,128)(2,1)} %param.10) | copy-start | bytes 1572868
  (25 other events, 24.9 us)
Sparse Core Ops, SparseCore 0:
  228.0 32.6 all-gather.1
  314.3 61.8 reduce-scatter.1
